TPU v7x, 512 devices: a whole 4x8x8 slice. The times are simulated.
512 devices in a mesh: seq: 32 (over y, x), head: 16 (over z, core).
Axes of the slice: x: 4, y: 8, z: 8, core: 2. Of those that a mesh axis runs over, the one named last changes fastest.
Arguments:
- features: bfloat16 [65536, 8192], P(('seq', 'head')), may hold values from -6 to 6
- increment_per_head: bfloat16 [65536, 128], P(('seq', 'head')), may hold values from 0.0049743652 to 0.049804688
- token_log_decay: bfloat16 [65536, 128], P(('seq', 'head')), may hold values from -2 to 0, as said below
- b_matrix: bfloat16 [65536, 1024], P(('seq', 'head')), may hold values from -6 to 6
- c_matrix: bfloat16 [65536, 1024], P(('seq', 'head')), may hold values from -0.5 to 0.5
- skip_gain: float32 [128], P('head'), may hold values from 0.5 to 1.5
Outputs:
- mixed_out: bfloat16 [65536, 8192], P(('seq', 'head'))
Inputs may be any that keep to these rules, and one draw needn't show every extreme that they name: `token_log_decay`: log decays are never positive.
All inputs are finite; a program needn't handle non-finite values.
Results may differ from a plain program's by a relative error of at most 0.01.
Values may be sent and summed in bfloat16 or wider, within the bound.
No kernel may reach another device: no remote copies, remote signals or barrier semaphores. Data moves between devices by JAX's collectives and lax.ppermute only.
A program may use at most 128 MiB of HBM per device.

v0:
```python
import jax
import jax.numpy as jnp
from jax import lax
from jax.sharding import PartitionSpec as P

G = 8
Q = 128


def prefix_2(value, axis, combine, identity):
    size, index = (lax.axis_size(axis), lax.axis_index(axis))
    everything = jax.tree.map(
        lambda part, kind: lax.all_gather(part.astype(kind), axis),
        value,
        (jnp.bfloat16, jnp.bfloat16),
    )
    start = jax.tree.map(
        lambda part, zero: jnp.broadcast_to(jnp.asarray(zero, part.dtype), part.shape),
        value,
        identity,
    )

    def lap(k, before):
        reached = k < index
        new = combine(
            before, jax.tree.map(lambda part, own: part[k].astype(own.dtype), everything, value)
        )
        return jax.tree.map(lambda a, b: jnp.where(reached, a, b), new, before)

    return lax.fori_loop(0, size, lap, start)


def combine(earlier, latter):
    return (earlier[0] + latter[0], jnp.exp(latter[0])[:, None, None] * earlier[1] + latter[1])


def local(features, increment_per_head, token_log_decay, b_matrix, c_matrix, skip_gain):
    n_groups = lax.axis_size("head")
    local_rows = features.shape[0]
    head_count = increment_per_head.shape[1]
    local_heads = head_count // n_groups
    head_width = features.shape[1] // head_count
    state_width = b_matrix.shape[1] // G
    b_slots = jnp.repeat(b_matrix.reshape(local_rows, G, state_width), n_groups // G, axis=1)
    c_slots = jnp.repeat(c_matrix.reshape(local_rows, G, state_width), n_groups // G, axis=1)
    local_groups = max(1, G // n_groups)
    per_group = local_heads // local_groups
    paired = jnp.concatenate([b_slots, c_slots], axis=2)
    rates = jnp.concatenate(
        [
            increment_per_head.reshape(local_rows, n_groups, local_heads),
            token_log_decay.reshape(local_rows, n_groups, local_heads),
        ],
        axis=2,
    )
    blocks_in = features.reshape(local_rows, n_groups, local_heads * head_width)
    moved_x, moved_rates, moved_bc = (
        lax.all_to_all(blocks_in, "head", split_axis=1, concat_axis=0, tiled=True),
        lax.all_to_all(rates, "head", split_axis=1, concat_axis=0, tiled=True),
        lax.all_to_all(paired, "head", split_axis=1, concat_axis=0, tiled=True),
    )
    token_count = local_rows * n_groups
    block_count = token_count // Q
    grouped_input_matrix = moved_x.reshape(block_count, Q, local_heads, head_width)
    step_local = (
        moved_rates[:, 0, :local_heads]
        .astype(jnp.float32)
        .reshape(block_count, Q, local_heads)
        .transpose(0, 2, 1)
    )
    shrinkage_within_segment = (
        moved_rates[:, 0, local_heads:]
        .astype(jnp.float32)
        .reshape(block_count, Q, local_heads)
        .transpose(0, 2, 1)
    )
    b_local = moved_bc[:, 0, : local_groups * state_width].reshape(
        block_count, Q, local_groups, state_width
    )
    c_local = moved_bc[:, 0, local_groups * state_width :].reshape(
        block_count, Q, local_groups, state_width
    )
    within = jnp.cumsum(shrinkage_within_segment, axis=2)
    block_total = within[:, :, -1]
    scores = jnp.einsum("ctgn,csgn->cgts", c_local, b_local, preferred_element_type=jnp.float32)
    scores = jnp.repeat(scores, per_group, axis=1)
    causal = (jnp.arange(Q)[:, None] >= jnp.arange(Q)[None, :])[None, None]
    gap_log = within[:, :, :, None] - within[:, :, None, :]
    damping = jnp.where(causal, jnp.exp(jnp.where(causal, gap_log, 0.0)), 0.0)
    weight = (scores * damping * step_local[:, :, None, :]).astype(jnp.bfloat16)
    inside = jnp.einsum(
        "chts,cshp->cthp", weight, grouped_input_matrix, preferred_element_type=jnp.float32
    )
    factor = (jnp.exp(block_total[:, :, None] - within) * step_local).transpose(0, 2, 1)
    scaled = (grouped_input_matrix * factor[..., None]).astype(jnp.bfloat16)
    update = jnp.einsum(
        "csgn,csgkp->cgknp",
        b_local,
        scaled.reshape(block_count, Q, local_groups, per_group, head_width),
        preferred_element_type=jnp.float32,
    ).reshape(block_count, local_heads, state_width, head_width)

    def advance(state_now, inputs):
        total_now, update_now = inputs
        return (jnp.exp(total_now)[:, None, None] * state_now + update_now, state_now)

    dev_state, local_carried = lax.scan(
        advance,
        jnp.zeros((local_heads, state_width, head_width), jnp.float32),
        (block_total, update),
    )
    prefix = jnp.cumsum(block_total, axis=0) - block_total
    dev_total = jnp.sum(block_total, axis=0)
    _, incoming = prefix_2(
        (dev_total, dev_state),
        "seq",
        combine,
        (jnp.zeros_like(dev_total), jnp.zeros_like(dev_state)),
    )
    carried = local_carried + jnp.exp(prefix)[:, :, None, None] * incoming[None]
    carried_in = carried.astype(jnp.bfloat16)
    outside = jnp.einsum(
        "ctgn,cgknp->ctgkp",
        c_local,
        carried_in.reshape(block_count, local_groups, per_group, state_width, head_width),
        preferred_element_type=jnp.float32,
    ).reshape(block_count, Q, local_heads, head_width)
    mixed = (
        inside
        + jnp.exp(within).transpose(0, 2, 1)[..., None] * outside
        + skip_gain[None, None, :, None] * grouped_input_matrix
    )
    leaving = mixed.astype(jnp.bfloat16).reshape(token_count, 1, local_heads * head_width)
    returned = lax.all_to_all(leaving, "head", split_axis=0, concat_axis=1, tiled=True)
    return returned.reshape(local_rows, head_count * head_width)


def solution(mesh):
    in_specs = (
        P(("seq", "head"), None),
        P(("seq", "head"), None),
        P(("seq", "head"), None),
        P(("seq", "head"), None),
        P(("seq", "head"), None),
        P("head"),
    )
    out_specs = P(("seq", "head"), None)
    return jax.shard_map(local, mesh=mesh, in_specs=in_specs, out_specs=out_specs, check_vma=False)
```

profile of v0, /device:TPU:1, one launch (start us, length us, event | category | flops | bytes accessed | tf_op | source)
XLA Modules:
  0.0 408.8 jit_solution(9127890750724101850)
XLA Ops:
  6.5 1.0 copy.52
  9.1 11.8 %all-to-all-start.1 = ((bf16[128,16,16]{0,2,1:T(8,128)(2,1)}), bf16[128,16,16]{0,2,1:T(8,128)(2,1)S(1)}, u32[]{:S(2)}, u32[]{:S(2)}) async-start(bf16[128,16,16]{0,2,1:T(8,128)(2,1)} %pad_maximum_fusion.1), calls=%async_computation.1 | async-start | bytes 131072 | tf_op jit(solution)/shard_map/all_to_all | solution.py:59
  21.0 1.0 copy_bitcast_fusion.1
  22.2 1.1 pad_maximum_fusion
  23.3 5.4 %all-to-all-done.1 = bf16[128,16,16]{0,2,1:T(8,128)(2,1)S(1)} async-done(((bf16[128,16,16]{0,2,1:T(8,128)(2,1)}), bf16[128,16,16]{0,2,1:T(8,128)(2,1)S(1)}, u32[]{:S(2)}, u32[]{:S(2)}) %all-to-all-start.1) | async-done | bytes 65568 | tf_op jit(solution)/shard_map/all_to_all | solution.py:59
  28.7 3.6 all-to-all-start
  32.3 2.4 copy.71
  34.8 25.5 %all-to-all-done = bf16[128,16,256]{2,0,1:T(8,128)(2,1)S(1)} async-done(((bf16[128,16,256]{2,0,1:T(8,128)(2,1)}), bf16[128,16,256]{2,0,1:T(8,128)(2,1)S(1)}, u32[]{:S(2)}, u32[]{:S(2)}) %all-to-all-start) | async-done | bytes 1048608 | tf_op jit(solution)/shard_map/all_to_all | solution.py:60
  60.3 1.0 copy-done.3
  61.4 3.6 all-to-all-start.2
  65.7 4.5 %reduce_window_sum.22 = f32[16,8,128]{2,1,0:T(8,128)S(1)} reduce-window(f32[16,8,128]{2,1,0:T(8,128)S(1)} %get-tuple-element.214, f32[]{:T(128)} %constant.47.clone.1), window={size=1x1x128 pad=0_0x0_0x127_0}, to_apply=%region_0.0 | reduce-window | flops 2080768 | bytes 131076 | tf_op jit(solution)/shard_map/jit(cumsum)/reduce_window_sum | solution.py:83
  70.7 2.1 fusion.20
  72.7 41.1 %all-to-all-done.2 = bf16[128,16,512]{0,2,1:T(8,128)(2,1)S(1)} async-done(((bf16[128,16,512]{0,2,1:T(8,128)(2,1)}), bf16[128,16,512]{0,2,1:T(8,128)(2,1)S(1)}, u32[]{:S(2)}, u32[]{:S(2)}) %all-to-all-start.2) | async-done | bytes 2097184 | tf_op jit(solution)/shard_map/all_to_all | solution.py:58
  113.8 4.1 convolution_bitcast_fusion
  117.9 34.9 %while.27 = (s32[]{:T(128)}, f32[8,128,64]{2,1,0:T(8,128)S(1)}, f32[16,8,128,64]{3,2,1,0:T(8,128)}, f32[16,8]{1,0:T(8,128)S(1)}, f32[16,8,128,64]{2,3,1,0:T(8,128)}, /*index=5*/s32[]{:T(128)}, s32[]{:T(128)}) while((s32[]{:T(128)}, f32[8,128,64]{2,1,0:T(8,128)S(1)}, f32[16,8,128,64]{3,2,1,0:T(8,128)}, f32[16,8]{1,0:T(8,128)S(1)}, ...), condition=%wide.region_2.3_spmd.clone, body=%wide.region_1.2_spmd.clone.sunk | while | flops 262147 | bytes 2621644 | solution.py:107
  118.7 1.0 constant_dynamic-slice_fusion.5
  120.9 1.0 constant_dynamic-slice_fusion.5
  123.1 1.0 constant_dynamic-slice_fusion.5
  125.3 1.0 constant_dynamic-slice_fusion.5
  127.4 1.0 constant_dynamic-slice_fusion.5
  129.6 1.0 constant_dynamic-slice_fusion.5
  131.8 1.0 constant_dynamic-slice_fusion.5
  134.0 1.0 constant_dynamic-slice_fusion.5
  136.1 1.0 constant_dynamic-slice_fusion.5
  138.3 1.0 constant_dynamic-slice_fusion.5
  140.5 1.0 constant_dynamic-slice_fusion.5
  142.7 1.0 constant_dynamic-slice_fusion.5
  144.9 1.0 constant_dynamic-slice_fusion.5
  147.1 1.0 constant_dynamic-slice_fusion.5
  149.2 1.0 constant_dynamic-slice_fusion.5
  151.4 1.0 constant_dynamic-slice_fusion.5
  153.6 1.3 dynamic-slice
  155.8 61.7 %all-reduce = bf16[256]{0:T(256)(128)(2,1)S(1)} all-reduce(bf16[256]{0:T(256)(128)(2,1)S(1)} %dynamic-update-slice), channel_id=2, replica_groups=mesh['seq'=32,'head'=16] {'seq'}, use_global_device_ids=true, to_apply=%add | all-reduce | flops 256 | bytes 1024
  217.6 2.6 fusion.21
  220.2 16.5 %all-gather.4.cloned.1.call-done = bf16[256,128,64]{1,2,0:T(8,128)(2,1)} async-done(((bf16[8,128,64]{1,2,0:T(8,128)(2,1)}), bf16[256,128,64]{1,2,0:T(8,128)(2,1)}) %all-gather.4.cloned.1.call-update) | async-done | bytes 4194320 | tf_op jit(solution)/shard_map/all_gather | solution.py:13
  236.7 41.5 %while.28 = (s32[]{:T(128)}, f32[8,128,64]{2,1,0:T(8,128)S(1)}, s32[]{:T(128)}, bf16[32,8]{1,0:T(8,128)(2,1)S(1)}, bf16[32,8,128,64]{2,3,1,0:T(8,128)(2,1)}, /*index=5*/s32[]{:T(128)}, s32[]{:T(128)}) while((s32[]{:T(128)}, f32[8,128,64]{2,1,0:T(8,128)S(1)}, s32[]{:T(128)}, bf16[32,8]{1,0:T(8,128)(2,1)S(1)}, ...), condition=%wide.region_6.7_spmd.clone, body=%wide.region_5.6_spmd.clone.sunk | while | flops 327692 | bytes 1179841 | solution.py:30
  238.0 0.9 constant_dynamic-slice_fusion.6
  239.3 0.9 constant_dynamic-slice_fusion.6
  240.6 0.9 constant_dynamic-slice_fusion.6
  241.9 0.9 constant_dynamic-slice_fusion.6
  243.2 0.9 constant_dynamic-slice_fusion.6
  244.5 0.9 constant_dynamic-slice_fusion.6
  245.8 0.9 constant_dynamic-slice_fusion.6
  251.0 0.9 constant_dynamic-slice_fusion.6
  252.3 0.9 constant_dynamic-slice_fusion.6
  257.5 0.9 constant_dynamic-slice_fusion.6
  258.8 0.9 constant_dynamic-slice_fusion.6
  264.0 0.9 constant_dynamic-slice_fusion.6
  265.3 0.9 constant_dynamic-slice_fusion.6
  269.1 0.9 constant_dynamic-slice_fusion.6
  270.4 0.9 constant_dynamic-slice_fusion.6
  275.6 0.9 constant_dynamic-slice_fusion.6
  276.9 0.9 constant_dynamic-slice_fusion.6
  278.3 6.0 %fusion.7 = f32[16,8,64,128]{3,2,1,0:T(8,128)S(1)} fusion(bf16[16,128,128,1]{2,1,3,0:T(8,128)(2,1)S(1)} %bitcast.127, f32[16,8,128,64]{3,2,1,0:T(8,128)} %get-tuple-element.127, f32[8,128,64]{2,1,0:T(8,128)S(1)} %get-tuple-element.129, f32[16,8]{1,0:T(8,128)S(1)} %subtract_exponential_fusion), kind=kOutput, calls=%fused_computation.18 | convolution fusion | flops 271581184 | bytes 9175552 | tf_op jit(solution)/shard_map/ctgn,cgknp->ctgkp/dot_general | solution.py:122
  284.3 4.2 %fusion.6 = bf16[16,128,8,64]{1,3,2,0:T(8,128)(2,1)S(1)} fusion(bf16[16,128,8,64]{1,3,2,0:T(8,128)(2,1)S(1)} %bitcast.123, f32[16,8,64,128]{3,2,1,0:T(8,128)S(1)} %fusion.7, f32[8]{0:T(128)S(1)} %copy-done.7, f32[16,128,8]{1,2,0:T(8,128)S(1)} %exponential_bitcast_fusion.1, f32[16,8,128]{2,1,0:T(8,128)S(1)} %copy-done.6, ...), kind=kOutput, calls=%fused_computation.17 | convolution fusion | flops 287309824 | bytes 9650208 | tf_op jit(solution)/shard_map/chts,cshp->cthp/dot_general | solution.py:91
  288.5 3.6 copy.76
  292.1 14.9 %reshape.157 = bf16[2048,1,512]{2,1,0:T(2,128)(2,1)} reshape(bf16[16,128,8,64]{3,2,1,0:T(8,128)(2,1)} %copy.76) | data formatting | bytes 4194304 | tf_op jit(solution)/shard_map/reshape | solution.py:133
  307.5 14.1 %reduce.1 = bf16[2048,512]{1,0:T(8,128)(2,1)S(1)} reduce(bf16[2048,1,512]{2,1,0:T(2,128)(2,1)} %reshape.157, bf16[]{:T(256)} %broadcast.37), dimensions={1}, to_apply=%reshape.157.reduce_sub_computation | reduce | bytes 4194306 | tf_op jit(solution)/shard_map/reshape | solution.py:133
  321.6 2.8 reshape.164
  324.3 61.7 %all_to_all.66 = bf16[16,2,32768]{2,1,0:T(2,128)(2,1)S(1)} all-to-all(bf16[16,2,32768]{2,1,0:T(2,128)(2,1)} %reshape.164), channel_id=1, replica_groups=mesh['seq'=32,'head'=16] {'head'}, dimensions={0} | all-to-all | bytes 4194304 | tf_op jit(solution)/shard_map/all_to_all | solution.py:134
  386.1 6.7 %reshape.165 = bf16[2048,1,512]{2,1,0:T(2,128)(2,1)} reshape(bf16[16,2,32768]{2,1,0:T(2,128)(2,1)S(1)} %all_to_all.66) | data formatting | bytes 4194304
  392.7 2.8 copy.80
  395.5 2.4 copy.66
  397.9 4.1 copy.67
  (214 shorter events, 47.9 us)
Async XLA Ops:
  6.5 14.4 %copy-start = (bf16[128,1024]{1,0:T(8,128)(2,1)S(1)}, bf16[128,1024]{1,0:T(8,128)(2,1)}, u32[]{:S(2)}) copy-start(bf16[128,1024]{1,0:T(8,128)(2,1)} %param.14) | copy-start | bytes 786436
  6.5 25.8 %copy-start.4 = (bf16[128,8192]{1,0:T(8,128)(2,1)S(1)}, bf16[128,8192]{1,0:T(8,128)(2,1)}, u32[]{:S(2)}) copy-start(bf16[128,8192]{1,0:T(8,128)(2,1)} %param.10) | copy-start | bytes 6291460
  9.1 19.6 %all-to-all-start.1 = ((bf16[128,16,16]{0,2,1:T(8,128)(2,1)}), bf16[128,16,16]{0,2,1:T(8,128)(2,1)S(1)}, u32[]{:S(2)}, u32[]{:S(2)}) async-start(bf16[128,16,16]{0,2,1:T(8,128)(2,1)} %pad_maximum_fusion.1), calls=%async_computation.1 | async-start | bytes 131072 | tf_op jit(solution)/shard_map/all_to_all | solution.py:59
  28.7 31.6 %all-to-all-start = ((bf16[128,16,256]{2,0,1:T(8,128)(2,1)}), bf16[128,16,256]{2,0,1:T(8,128)(2,1)S(1)}, u32[]{:S(2)}, u32[]{:S(2)}) async-start(bf16[128,16,256]{2,0,1:T(8,128)(2,1)} %pad_maximum_fusion), calls=%async_computation | async-start | bytes 2097152 | tf_op jit(solution)/shard_map/all_to_all | solution.py:60
  60.3 1.0 copy-start.3
  61.4 52.5 %all-to-all-start.2 = ((bf16[128,16,512]{0,2,1:T(8,128)(2,1)}), bf16[128,16,512]{0,2,1:T(8,128)(2,1)S(1)}, u32[]{:S(2)}, u32[]{:S(2)}) async-start(bf16[128,16,512]{0,2,1:T(8,128)(2,1)} %bitcast.124), calls=%async_computation.2 | async-start | bytes 4194304 | tf_op jit(solution)/shard_map/all_to_all | solution.py:58
  65.0 171.8 %all-gather.4.cloned.1.call-start = ((), (), s32[]{:S(2)}) async-start(), calls=%async_computation.4 | async-start | bytes 4325376 | tf_op jit(solution)/shard_map/all_gather | solution.py:13
  113.8 4.1 copy-start.1
  278.2 6.0 %copy-start.2 = (bf16[128,16,512]{0,2,1:T(8,128)(2,1)S(1)}, bf16[128,16,512]{0,2,1:T(8,128)(2,1)}, u32[]{:S(2)}) copy-start(bf16[128,16,512]{0,2,1:T(8,128)(2,1)} %copy-done.1) | copy-start | bytes 6291460
  278.2 6.0 %copy-start.5 = (f32[16,128,128]{2,1,0:T(8,128)S(1)}, f32[16,128,128]{2,1,0:T(8,128)}, u32[]{:S(2)}) copy-start(f32[16,128,128]{2,1,0:T(8,128)} %fusion.21) | copy-start | bytes 3145732
  278.2 6.0 %copy-start.6 = (f32[16,8,128]{2,1,0:T(8,128)S(1)}, f32[16,8,128]{2,1,0:T(8,128)}, u32[]{:S(2)}) copy-start(f32[16,8,128]{2,1,0:T(8,128)} %get-tuple-element.213) | copy-start | bytes 196612
  278.2 6.0 %copy-start.7 = (f32[8]{0:T(128)S(1)}, f32[8]{0:T(128)}, u32[]{:S(2)}) copy-start(f32[8]{0:T(128)} %param.15) | copy-start | bytes 100
Sparse Core Ops, SparseCore 0:
  153.7 83.0 all-gather.3
where the time goes:
time: 411 us; the launch traced here: 409 us
  blocking collectives  123 us (30%)
  local copies, waits for them, and re-layouts  103 us (25%)
  waiting for transfers between devices  88.6 us (22%)
  other arithmetic  41.7 us (10%)
  starting transfers between devices  19.1 us (5%)
  matrix products  16.8 us (4%)
  between operations  14.3 us (3%)
    all_to_all x1, blocking collectives, local(): lax.all_to_all(leaving, 'head', split_axis=0, concat_axis=1, tiled=True)  61.7 us
    unnamed x1, blocking collectives  61.7 us
    all_to_all x1, waiting for transfers between devices, local(): lax.all_to_all(blocks_in, 'head', split_axis=1, concat_axis=0, tiled=True)  41.1 us
    dynamic_slice x64, local copies, waits for them, and re-layouts, lap(): part[k].astype(own.dtype)  35.1 us
    all_to_all x1, waiting for transfers between devices, local(): lax.all_to_all(paired, 'head', split_axis=1, concat_axis=0, tiled=True)  25.5 us
    reshape x3, local copies, waits for them, and re-layouts, local(): mixed.astype(jnp.bfloat16).reshape(token_count, 1, local_heads * head_width)  19 us
    dynamic_slice x32, local copies, waits for them, and re-layouts, local(): lax.scan(advance, jnp.zeros((local_heads, state_width, head_width), jnp.f...  18.7 us
    unnamed x24, local copies, waits for them, and re-layouts  16.7 us
  transfers between devices with their start and end apart: 4, of which 4 were waited for; matrix products, arithmetic and copies ran while one was open for 4% of the time, Pallas kernels for 0%

commit v1 on v0

--- a/solution.py
+++ b/solution.py
@@ -131,7 +131,10 @@
         + skip_gain[None, None, :, None] * grouped_input_matrix
     )
     leaving = mixed.astype(jnp.bfloat16).reshape(token_count, 1, local_heads * head_width)
-    returned = lax.all_to_all(leaving, "head", split_axis=0, concat_axis=1, tiled=True)
+    count = lax.axis_size("head")
+    blocks = jnp.stack(jnp.split(leaving, count, axis=0), axis=0)
+    blocks = lax.all_to_all(blocks, "head", split_axis=0, concat_axis=0)
+    returned = jnp.concatenate(blocks, axis=1)
     return returned.reshape(local_rows, head_count * head_width)
 
 

time: 411 us -> 362 us (0.88)
  local copies, waits for them, and re-layouts: 103 us -> 68.6 us
  other arithmetic: 41.7 us -> 27.8 us
    reshape x4 -> x0, local copies, waits for them, and re-layouts: 23.1 us -> none  [the longest x3 19 us: local(): mixed.astype(jnp.bfloat16).reshape(token_count, 1, local_heads * head_width)]
    reshape x1 -> x0, other arithmetic: 14.1 us -> none  [local(): mixed.astype(jnp.bfloat16).reshape(token_count, 1, local_heads * head_width)]
    unnamed x24 -> x38, local copies, waits for them, and re-layouts: 16.7 us -> 4.68 us
where the time goes in v1:
time: 362 us; the launch traced here: 360 us
  blocking collectives  123 us (34%)
  waiting for transfers between devices  89.7 us (25%)
  local copies, waits for them, and re-layouts  68.6 us (19%)
  other arithmetic  27.8 us (8%)
  starting transfers between devices  19.1 us (5%)
  matrix products  15.8 us (4%)
  between operations  14.4 us (4%)
    unnamed x1, blocking collectives  61.7 us
    all_to_all x1, blocking collectives, local(): blocks = lax.all_to_all(blocks, 'head', split_axis=0, concat_axis=0)  61.5 us
    all_to_all x1, waiting for transfers between devices, local(): lax.all_to_all(blocks_in, 'head', split_axis=1, concat_axis=0, tiled=True)  41.1 us
    dynamic_slice x64, local copies, waits for them, and re-layouts, lap(): part[k].astype(own.dtype)  35.1 us
    all_to_all x1, waiting for transfers between devices, local(): lax.all_to_all(paired, 'head', split_axis=1, concat_axis=0, tiled=True)  25.5 us
    dynamic_slice x32, local copies, waits for them, and re-layouts, local(): lax.scan(advance, jnp.zeros((local_heads, state_width, head_width), jnp.f...  18.7 us
    all_gather x1, waiting for transfers between devices, prefix_2(): lax.all_gather(part.astype(kind), axis)  17.7 us
    dynamic_update_slice x16, other arithmetic, local(): lax.scan(advance, jnp.zeros((local_heads, state_width, head_width), jnp.f...  13.6 us
  transfers between devices with their start and end apart: 4, of which 4 were waited for; matrix products, arithmetic and copies ran while one was open for 4% of the time, Pallas kernels for 0%

profile of v1, /device:TPU:1, one launch (start us, length us, event | category | flops | bytes accessed | tf_op | source)
XLA Modules:
  0.0 360.4 jit_solution(12915998516612345840)
XLA Ops:
  9.0 11.8 %all-to-all-start.1 = ((bf16[128,16,16]{0,2,1:T(8,128)(2,1)}), bf16[128,16,16]{0,2,1:T(8,128)(2,1)S(1)}, u32[]{:S(2)}, u32[]{:S(2)}) async-start(bf16[128,16,16]{0,2,1:T(8,128)(2,1)} %pad_maximum_fusion.1), calls=%async_computation.1 | async-start | bytes 131072 | tf_op jit(solution)/shard_map/all_to_all | solution.py:59
  20.9 1.0 copy_bitcast_fusion.1
  22.1 1.1 pad_maximum_fusion
  23.2 5.4 %all-to-all-done.1 = bf16[128,16,16]{0,2,1:T(8,128)(2,1)S(1)} async-done(((bf16[128,16,16]{0,2,1:T(8,128)(2,1)}), bf16[128,16,16]{0,2,1:T(8,128)(2,1)S(1)}, u32[]{:S(2)}, u32[]{:S(2)}) %all-to-all-start.1) | async-done | bytes 65568 | tf_op jit(solution)/shard_map/all_to_all | solution.py:59
  28.6 3.6 all-to-all-start
  32.2 2.4 copy.51
  34.7 25.5 %all-to-all-done = bf16[128,16,256]{2,0,1:T(8,128)(2,1)S(1)} async-done(((bf16[128,16,256]{2,0,1:T(8,128)(2,1)}), bf16[128,16,256]{2,0,1:T(8,128)(2,1)S(1)}, u32[]{:S(2)}, u32[]{:S(2)}) %all-to-all-start) | async-done | bytes 1048608 | tf_op jit(solution)/shard_map/all_to_all | solution.py:60
  60.2 1.1 copy-done.4
  61.3 3.6 %all-to-all-start.2 = ((bf16[128,16,512]{0,2,1:T(8,128)(2,1)}), bf16[128,16,512]{0,2,1:T(8,128)(2,1)S(1)}, u32[]{:S(2)}, u32[]{:S(2)}) async-start(bf16[128,16,512]{0,2,1:T(8,128)(2,1)} %bitcast.168), calls=%async_computation.2 | async-start | bytes 4194304 | tf_op jit(solution)/shard_map/all_to_all | solution.py:58
  65.6 4.5 %reduce_window_sum.22 = f32[16,8,128]{2,1,0:T(8,128)S(1)} reduce-window(f32[16,8,128]{2,1,0:T(8,128)S(1)} %get-tuple-element.225, f32[]{:T(128)} %constant.47.clone.1), window={size=1x1x128 pad=0_0x0_0x127_0}, to_apply=%region_0.0 | reduce-window | flops 2080768 | bytes 131076 | tf_op jit(solution)/shard_map/jit(cumsum)/reduce_window_sum | solution.py:83
  70.6 2.1 fusion.21
  72.7 41.1 %all-to-all-done.2 = bf16[128,16,512]{0,2,1:T(8,128)(2,1)S(1)} async-done(((bf16[128,16,512]{0,2,1:T(8,128)(2,1)}), bf16[128,16,512]{0,2,1:T(8,128)(2,1)S(1)}, u32[]{:S(2)}, u32[]{:S(2)}) %all-to-all-start.2) | async-done | bytes 2097184 | tf_op jit(solution)/shard_map/all_to_all | solution.py:58
  113.7 4.1 %convolution_bitcast_fusion = f32[16,8,128,64]{2,3,1,0:T(8,128)} fusion(bf16[16,128,128,1]{2,1,3,0:T(8,128)(2,1)} %bitcast.172, bf16[16,128,8,64]{1,3,2,0:T(8,128)(2,1)S(1)} %bitcast.166, f32[16,128,8]{1,2,0:T(8,128)S(1)} %convert_multiply_fusion.2), kind=kOutput, calls=%fused_computation.29 | convolution fusion | flops 271581184 | bytes 6881280 | tf_op jit(solution)/shard_map/csgn,csgkp->cgknp/dot_general | solution.py:96
  117.8 35.0 %while.27 = (s32[]{:T(128)}, f32[8,128,64]{2,1,0:T(8,128)S(1)}, f32[16,8,128,64]{3,2,1,0:T(8,128)}, f32[16,8]{1,0:T(8,128)S(1)}, f32[16,8,128,64]{2,3,1,0:T(8,128)}, /*index=5*/s32[]{:T(128)}, s32[]{:T(128)}) while((s32[]{:T(128)}, f32[8,128,64]{2,1,0:T(8,128)S(1)}, f32[16,8,128,64]{3,2,1,0:T(8,128)}, f32[16,8]{1,0:T(8,128)S(1)}, ...), condition=%wide.region_2.3_spmd.clone, body=%wide.region_1.2_spmd.clone.sunk | while | flops 262147 | bytes 2621644 | solution.py:107
  118.6 1.0 constant_dynamic-slice_fusion.5
  120.8 1.0 constant_dynamic-slice_fusion.5
  123.0 1.0 constant_dynamic-slice_fusion.5
  125.2 1.0 constant_dynamic-slice_fusion.5
  127.4 1.0 constant_dynamic-slice_fusion.5
  129.6 1.0 constant_dynamic-slice_fusion.5
  131.8 1.0 constant_dynamic-slice_fusion.5
  134.0 1.0 constant_dynamic-slice_fusion.5
  136.1 1.0 constant_dynamic-slice_fusion.5
  138.3 1.0 constant_dynamic-slice_fusion.5
  140.5 1.0 constant_dynamic-slice_fusion.5
  142.7 1.0 constant_dynamic-slice_fusion.5
  144.9 1.0 constant_dynamic-slice_fusion.5
  147.1 1.0 constant_dynamic-slice_fusion.5
  149.2 1.0 constant_dynamic-slice_fusion.5
  151.5 1.0 constant_dynamic-slice_fusion.5
  153.6 1.3 dynamic-slice
  155.8 61.7 %all-reduce = bf16[256]{0:T(256)(128)(2,1)S(1)} all-reduce(bf16[256]{0:T(256)(128)(2,1)S(1)} %dynamic-update-slice), channel_id=2, replica_groups=mesh['seq'=32,'head'=16] {'seq'}, use_global_device_ids=true, to_apply=%add | all-reduce | flops 256 | bytes 1024
  217.6 1.5 fusion.22
  219.1 17.7 %all-gather.4.cloned.1.call-done = bf16[256,128,64]{1,2,0:T(8,128)(2,1)} async-done(((bf16[8,128,64]{1,2,0:T(8,128)(2,1)}), bf16[256,128,64]{1,2,0:T(8,128)(2,1)}) %all-gather.4.cloned.1.call-update) | async-done | bytes 4194320 | tf_op jit(solution)/shard_map/all_gather | solution.py:13
  236.8 41.5 %while.28 = (s32[]{:T(128)}, f32[8,128,64]{2,1,0:T(8,128)S(1)}, s32[]{:T(128)}, bf16[32,8]{1,0:T(8,128)(2,1)S(1)}, bf16[32,8,128,64]{2,3,1,0:T(8,128)(2,1)}, /*index=5*/s32[]{:T(128)}, s32[]{:T(128)}) while((s32[]{:T(128)}, f32[8,128,64]{2,1,0:T(8,128)S(1)}, s32[]{:T(128)}, bf16[32,8]{1,0:T(8,128)(2,1)S(1)}, ...), condition=%wide.region_6.7_spmd.clone, body=%wide.region_5.6_spmd.clone.sunk | while | flops 327692 | bytes 1179841 | solution.py:30
  238.1 0.9 constant_dynamic-slice_fusion.6
  239.4 0.9 constant_dynamic-slice_fusion.6
  240.7 0.9 constant_dynamic-slice_fusion.6
  242.0 0.9 constant_dynamic-slice_fusion.6
  243.3 0.9 constant_dynamic-slice_fusion.6
  244.6 0.9 constant_dynamic-slice_fusion.6
  245.9 0.9 constant_dynamic-slice_fusion.6
  247.2 0.9 constant_dynamic-slice_fusion.6
  248.5 0.9 constant_dynamic-slice_fusion.6
  249.8 0.9 constant_dynamic-slice_fusion.6
  251.1 0.9 constant_dynamic-slice_fusion.6
  252.4 0.9 constant_dynamic-slice_fusion.6
  253.7 0.9 constant_dynamic-slice_fusion.6
  255.0 0.9 constant_dynamic-slice_fusion.6
  256.3 0.9 constant_dynamic-slice_fusion.6
  257.5 0.9 constant_dynamic-slice_fusion.6
  258.8 0.9 constant_dynamic-slice_fusion.6
  260.1 0.9 constant_dynamic-slice_fusion.6
  261.4 0.9 constant_dynamic-slice_fusion.6
  262.7 0.9 constant_dynamic-slice_fusion.6
  264.0 0.9 constant_dynamic-slice_fusion.6
  266.6 0.9 constant_dynamic-slice_fusion.6
  267.9 0.9 constant_dynamic-slice_fusion.6
  273.1 0.9 constant_dynamic-slice_fusion.6
  274.4 0.9 constant_dynamic-slice_fusion.6
  278.3 6.0 %fusion.7 = f32[16,8,64,128]{3,2,1,0:T(8,128)S(1)} fusion(bf16[16,128,128,1]{2,1,3,0:T(8,128)(2,1)S(1)} %bitcast.171, f32[16,8,128,64]{3,2,1,0:T(8,128)} %get-tuple-element.127, f32[8,128,64]{2,1,0:T(8,128)S(1)} %get-tuple-element.129, f32[16,8]{1,0:T(8,128)S(1)} %subtract_exponential_fusion), kind=kOutput, calls=%fused_computation.18 | convolution fusion | flops 271581184 | bytes 9175552 | tf_op jit(solution)/shard_map/ctgn,cgknp->ctgkp/dot_general | solution.py:122
  284.4 4.2 %fusion.6 = bf16[16,128,8,64]{1,3,2,0:T(8,128)(2,1)S(1)} fusion(bf16[16,128,8,64]{1,3,2,0:T(8,128)(2,1)S(1)} %bitcast.167, f32[16,8,64,128]{3,2,1,0:T(8,128)S(1)} %fusion.7, f32[8]{0:T(128)S(1)} %copy-done.8, f32[16,128,8]{1,2,0:T(8,128)S(1)} %exponential_bitcast_fusion.1, f32[16,8,128]{2,1,0:T(8,128)S(1)} %copy-done.7, ...), kind=kOutput, calls=%fused_computation.17 | convolution fusion | flops 287309824 | bytes 9650208 | tf_op jit(solution)/shard_map/chts,cshp->cthp/dot_general | solution.py:91
  289.2 61.5 %all_to_all.56 = bf16[16,128,1,512]{1,3,2,0:T(8,128)(2,1)S(1)} all-to-all(bf16[16,128,1,512]{1,3,2,0:T(8,128)(2,1)S(1)} %bitcast_dynamic-update-slice_fusion.1), channel_id=1, replica_groups=mesh['seq'=32,'head'=16] {'head'}, dimensions={0} | all-to-all | bytes 4194304 | tf_op jit(solution)/shard_map/all_to_all | solution.py:136
  350.7 2.9 copy.56
  (225 shorter events, 41.6 us)
Async XLA Ops:
  6.5 14.3 %copy-start = (bf16[128,1024]{1,0:T(8,128)(2,1)S(1)}, bf16[128,1024]{1,0:T(8,128)(2,1)}, u32[]{:S(2)}) copy-start(bf16[128,1024]{1,0:T(8,128)(2,1)} %param.14) | copy-start | bytes 786436
  9.0 19.6 %all-to-all-start.1 = ((bf16[128,16,16]{0,2,1:T(8,128)(2,1)}), bf16[128,16,16]{0,2,1:T(8,128)(2,1)S(1)}, u32[]{:S(2)}, u32[]{:S(2)}) async-start(bf16[128,16,16]{0,2,1:T(8,128)(2,1)} %pad_maximum_fusion.1), calls=%async_computation.1 | async-start | bytes 131072 | tf_op jit(solution)/shard_map/all_to_all | solution.py:59
  22.1 10.1 %copy-start.5 = (bf16[128,8192]{1,0:T(8,128)(2,1)S(1)}, bf16[128,8192]{1,0:T(8,128)(2,1)}, u32[]{:S(2)}) copy-start(bf16[128,8192]{1,0:T(8,128)(2,1)} %param.10) | copy-start | bytes 6291460
  28.6 31.6 %all-to-all-start = ((bf16[128,16,256]{2,0,1:T(8,128)(2,1)}), bf16[128,16,256]{2,0,1:T(8,128)(2,1)S(1)}, u32[]{:S(2)}, u32[]{:S(2)}) async-start(bf16[128,16,256]{2,0,1:T(8,128)(2,1)} %pad_maximum_fusion), calls=%async_computation | async-start | bytes 2097152 | tf_op jit(solution)/shard_map/all_to_all | solution.py:60
  60.2 1.1 copy-start.4
  61.3 52.5 %all-to-all-start.2 = ((bf16[128,16,512]{0,2,1:T(8,128)(2,1)}), bf16[128,16,512]{0,2,1:T(8,128)(2,1)S(1)}, u32[]{:S(2)}, u32[]{:S(2)}) async-start(bf16[128,16,512]{0,2,1:T(8,128)(2,1)} %bitcast.168), calls=%async_computation.2 | async-start | bytes 4194304 | tf_op jit(solution)/shard_map/all_to_all | solution.py:58
  64.9 171.9 %all-gather.4.cloned.1.call-start = ((), (), s32[]{:S(2)}) async-start(), calls=%async_computation.4 | async-start | bytes 4325376 | tf_op jit(solution)/shard_map/all_gather | solution.py:13
  113.7 4.1 %copy-start.1 = (bf16[128,16,512]{0,2,1:T(8,128)(2,1)}, bf16[128,16,512]{0,2,1:T(8,128)(2,1)S(1)}, u32[]{:S(2)}) copy-start(bf16[128,16,512]{0,2,1:T(8,128)(2,1)S(1)} %all-to-all-done.2) | copy-start | bytes 6291460
  117.8 99.8 %copy-start.3 = (bf16[2048,1,128]{2,0,1:T(8,128)(2,1)S(1)}, bf16[2048,1,128]{2,0,1:T(8,128)(2,1)}, u32[]{:S(2)}) copy-start(bf16[2048,1,128]{2,0,1:T(8,128)(2,1)} %get-tuple-element.222) | copy-start | bytes 1572868
  278.3 6.0 %copy-start.2 = (bf16[128,16,512]{0,2,1:T(8,128)(2,1)S(1)}, bf16[128,16,512]{0,2,1:T(8,128)(2,1)}, u32[]{:S(2)}) copy-start(bf16[128,16,512]{0,2,1:T(8,128)(2,1)} %copy-done.1) | copy-start | bytes 6291460
  278.3 6.0 %copy-start.6 = (f32[16,128,128]{2,1,0:T(8,128)S(1)}, f32[16,128,128]{2,1,0:T(8,128)}, u32[]{:S(2)}) copy-start(f32[16,128,128]{2,1,0:T(8,128)} %fusion.22) | copy-start | bytes 3145732
  278.3 6.0 %copy-start.7 = (f32[16,8,128]{2,1,0:T(8,128)S(1)}, f32[16,8,128]{2,1,0:T(8,128)}, u32[]{:S(2)}) copy-start(f32[16,8,128]{2,1,0:T(8,128)} %get-tuple-element.224) | copy-start | bytes 196612
  278.3 6.0 %copy-start.8 = (f32[8]{0:T(128)S(1)}, f32[8]{0:T(128)}, u32[]{:S(2)}) copy-start(f32[8]{0:T(128)} %param.15) | copy-start | bytes 100
Sparse Core Ops, SparseCore 0:
  153.7 83.0 all-gather.3
